TPU v7x, 256 devices: a whole 4x4x8 slice. The times are simulated.
256 devices in a mesh: req: 32 (over x, z), mlp: 8 (over y, core).
Axes of the slice: x: 4, y: 4, z: 8, core: 2. Of those that a mesh axis runs over, the one named last changes fastest.
Arguments:
- x_pages: bfloat16 [1024, 8, 4096], P('req', None, 'mlp'), may hold values from -6 to 6
- page_owner: int32 [1024], P('req'), may hold values from 0 to 31, as said below
- request_id: int32 [8192], P('req'), may hold values from 0 to 8191, as said below
- adapter_table: int32 [8192], P('req'), may hold values from 0 to 63
- ln_gain: float32 [4096], replicated, may hold values from 0.5 to 1.5
- ln_bias: float32 [4096], replicated, may hold values from -3 to 3
- w_query: bfloat16 [4096, 2048], P('req', 'mlp'), may hold values from -0.09375 to 0.09375
- w_key: bfloat16 [4096, 2048], P('req', 'mlp'), may hold values from -0.09375 to 0.09375
- w_value: bfloat16 [4096, 2048], P('req', 'mlp'), may hold values from -0.09375 to 0.09375
- w_attn_out: bfloat16 [2048, 4096], P('mlp', 'req'), may hold values from -0.125 to 0.125
- down_query: bfloat16 [4096, 1024], P('mlp'), may hold values from -0.09375 to 0.09375
- up_query: bfloat16 [1024, 2048], P(None, 'mlp'), may hold values from -1.5 to 1.5
- down_value: bfloat16 [4096, 1024], P('mlp'), may hold values from -0.09375 to 0.09375
- up_value: bfloat16 [1024, 2048], P(None, 'mlp'), may hold values from -1.5 to 1.5
- w_fc_in: bfloat16 [4096, 8192], P('req', 'mlp'), may hold values from -0.09375 to 0.09375
- b_fc_in: float32 [8192], P('mlp'), may hold values from -3 to 3
- down_fc: bfloat16 [4096, 1024], P('mlp'), may hold values from -0.09375 to 0.09375
- up_fc: bfloat16 [1024, 8192], P(None, 'mlp'), may hold values from -1.5 to 1.5
- w_fc_out: bfloat16 [8192, 4096], P('mlp', 'req'), may hold values from -0.0625 to 0.0625
- b_fc_out: float32 [4096], P('mlp'), may hold values from -3 to 3
Outputs:
- out_pages: bfloat16 [1024, 8, 4096], P('req', None, 'mlp')
Inputs may be any that keep to these rules, and one draw needn't show every extreme that they name: `page_owner`: every owner receives exactly 32 pages, at most 2 of them from one device, and some device sends exactly 2 pages to some owner. `request_id`: ids never fall; every request lies inside one owner's block of 256 rows, and the ids of block k lie in k * 256 to k * 256 + 255; some request is 256 long.
All inputs are finite; a program needn't handle non-finite values.
Results may differ from a plain program's by a relative error of at most 0.006.
Values may be sent and summed in bfloat16 or wider, within the bound.
No kernel may reach another device: no remote copies, remote signals or barrier semaphores. Data moves between devices by JAX's collectives and lax.ppermute only.
A program may use at most 128 MiB of HBM per device.

v0:
```python
import jax
import jax.numpy as jnp
from jax import lax
from jax.sharding import PartitionSpec as P

HS = 256
ROT = 64
NAD = 64
R = 16
EPS = 1e-05


def gelu_tanh(v):
    return 0.5 * v * (1.0 + jnp.tanh(0.7978845608028654 * (v + 0.044715 * v * v * v)))


def rotate(block, pos):
    half = ROT // 2
    freq = jnp.power(10000.0, -jnp.arange(half).astype(jnp.float32) * 2.0 / ROT)
    angle = pos.astype(jnp.float32)[:, None, None] * freq[None, None, :]
    cosine = jnp.cos(angle)
    sine = jnp.sin(angle)
    even = block[:, :, 0:ROT:2]
    odd = block[:, :, 1:ROT:2]
    turned = jnp.stack([even * cosine - odd * sine, odd * cosine + even * sine], axis=-1)
    turned = turned.reshape(block.shape[0], block.shape[1], ROT)
    return jnp.concatenate([turned, block[:, :, ROT:]], axis=2)


def on_device(
    x_pages,
    page_owner,
    request_id,
    adapter_table,
    ln_gain,
    ln_bias,
    w_query,
    w_key,
    w_value,
    w_attn_out,
    down_query,
    up_query,
    down_value,
    up_value,
    w_fc_in,
    b_fc_in,
    down_fc,
    up_fc,
    w_fc_out,
    b_fc_out,
):
    groups = lax.axis_size("req")
    pg_dev = x_pages.shape[0]
    page_len = x_pages.shape[1]
    width_m = x_pages.shape[2]
    tok = request_id.shape[0]
    per_owner = pg_dev // groups + 1
    slots = groups * per_owner
    page_iota = jnp.arange(pg_dev)
    earlier = (page_owner[None, :] == page_owner[:, None]) & (
        page_iota[None, :] < page_iota[:, None]
    )
    rank = jnp.sum(earlier.astype(jnp.int32), axis=1)
    slot = page_owner * per_owner + rank
    place = (slot[None, :] == jnp.arange(slots)[:, None]).astype(jnp.bfloat16)
    flat_pages = x_pages.reshape(pg_dev, page_len * width_m)
    outgoing = jnp.dot(place, flat_pages, preferred_element_type=jnp.float32).astype(jnp.bfloat16)
    outgoing = outgoing.reshape(groups, per_owner, page_len * width_m)
    filled = jnp.sum(place, axis=1).reshape(groups, per_owner)
    arrived, marks = (
        lax.all_to_all(outgoing, "req", split_axis=0, concat_axis=0, tiled=True),
        lax.all_to_all(filled, "req", split_axis=0, concat_axis=0, tiled=True),
    )
    valid = marks.reshape(slots).astype(jnp.float32)
    position = jnp.cumsum(valid) - 1.0
    take = (
        (position[None, :] == jnp.arange(pg_dev).astype(jnp.float32)[:, None])
        & (valid[None, :] > 0.5)
    ).astype(jnp.bfloat16)
    own_x = jnp.dot(
        take, arrived.reshape(slots, page_len * width_m), preferred_element_type=jnp.float32
    )
    own_x = own_x.astype(jnp.bfloat16).reshape(tok, width_m)
    column = lax.axis_index("mlp") * width_m
    whole = lax.all_gather(own_x, "mlp", axis=1, tiled=True).astype(jnp.float32)
    mean = jnp.mean(whole, axis=1, keepdims=True)
    var = jnp.mean(jnp.square(whole - mean), axis=1, keepdims=True)
    full_ln = ((whole - mean) * lax.rsqrt(var + EPS) * ln_gain + ln_bias).astype(jnp.bfloat16)
    ln_m = lax.dynamic_slice_in_dim(full_ln, column, width_m, 1)
    local_req = request_id - lax.axis_index("req") * tok
    lookup = local_req[:, None] == jnp.arange(tok)[None, :]
    adapter = jnp.sum(jnp.where(lookup, adapter_table[None, :], 0), axis=1)
    onehot = (adapter[:, None] == jnp.arange(NAD)[None, :]).astype(jnp.float32)
    onehot_low = onehot.astype(jnp.bfloat16)

    def pick(down):
        spread = jnp.dot(ln_m, down, preferred_element_type=jnp.float32).reshape(tok, NAD, R)
        return jnp.sum(spread * onehot[:, :, None], axis=1)

    picked = lax.psum((pick(down_query), pick(down_value), pick(down_fc)), "mlp")

    def lift(chosen, up):
        expanded = (onehot_low[:, :, None] * chosen.astype(jnp.bfloat16)[:, None, :]).reshape(
            tok, NAD * R
        )
        return jnp.dot(expanded, up, preferred_element_type=jnp.float32)

    row_iota = jnp.arange(tok)
    start = jnp.sum((request_id[None, :] < request_id[:, None]).astype(jnp.int32), axis=1)
    pos = row_iota - start
    mask = (request_id[:, None] == request_id[None, :]) & (row_iota[None, :] <= row_iota[:, None])
    heads_w = w_query.shape[1]
    pieces = (
        lax.all_gather(w_query, "req", axis=0, tiled=True),
        lax.all_gather(w_key, "req", axis=0, tiled=True),
        lax.all_gather(w_value, "req", axis=0, tiled=True),
    )
    cols = full_ln
    base_q, base_k, base_v = tuple(
        [jnp.dot(cols, piece, preferred_element_type=jnp.float32) for piece in pieces]
    )
    query = rotate(
        (base_q + lift(picked[0], up_query)).reshape(tok, heads_w // HS, HS), pos
    ).astype(jnp.bfloat16)
    keys = rotate(base_k.reshape(tok, heads_w // HS, HS), pos).astype(jnp.bfloat16)
    value = (
        (base_v + lift(picked[1], up_value)).astype(jnp.bfloat16).reshape(tok, heads_w // HS, HS)
    )
    scores = jnp.einsum("qhd,khd->hqk", query, keys, preferred_element_type=jnp.float32) * HS ** (
        -0.5
    )
    scores = jnp.where(mask[None, :, :], scores, -1e30)
    top = jnp.max(scores, axis=2, keepdims=True)
    weights = jnp.exp(scores - top)
    probs = (weights / jnp.sum(weights, axis=2, keepdims=True)).astype(jnp.bfloat16)
    mixed_heads = jnp.einsum("hqk,khd->qhd", probs, value, preferred_element_type=jnp.float32)
    attn = mixed_heads.astype(jnp.bfloat16).reshape(tok, heads_w)
    cols = full_ln
    hidden_pre = jnp.dot(
        cols, lax.all_gather(w_fc_in, "req", axis=0, tiled=True), preferred_element_type=jnp.float32
    )
    hidden_pre = hidden_pre + lift(picked[2], up_fc) + b_fc_in
    hidden = gelu_tanh(hidden_pre).astype(jnp.bfloat16)
    pieces = (
        lax.all_gather(w_attn_out, "req", axis=1, tiled=True),
        lax.all_gather(w_fc_out, "req", axis=1, tiled=True),
    )
    part = jnp.dot(attn, pieces[0], preferred_element_type=jnp.float32) + jnp.dot(
        hidden, pieces[1], preferred_element_type=jnp.float32
    )
    shares = lax.psum_scatter(part, "mlp", scatter_dimension=1, tiled=True)
    result = (own_x.astype(jnp.float32) + shares + b_fc_out).astype(jnp.bfloat16)
    back_flat = result.reshape(pg_dev, page_len * width_m)
    leaving = jnp.dot(take.T, back_flat, preferred_element_type=jnp.float32).astype(jnp.bfloat16)
    leaving = leaving.reshape(groups, per_owner, page_len * width_m)
    returned = lax.all_to_all(leaving, "req", split_axis=0, concat_axis=0, tiled=True)
    pages_back = jnp.dot(
        place.T, returned.reshape(slots, page_len * width_m), preferred_element_type=jnp.float32
    )
    return pages_back.astype(jnp.bfloat16).reshape(pg_dev, page_len, width_m)


def solution(mesh):
    in_specs = (
        P("req", None, "mlp"),
        P("req"),
        P("req"),
        P("req"),
        P(),
        P(),
        P("req", "mlp"),
        P("req", "mlp"),
        P("req", "mlp"),
        P("mlp", "req"),
        P("mlp", None),
        P(None, "mlp"),
        P("mlp", None),
        P(None, "mlp"),
        P("req", "mlp"),
        P("mlp"),
        P("mlp", None),
        P(None, "mlp"),
        P("mlp", "req"),
        P("mlp"),
    )
    out_specs = P("req", None, "mlp")
    return jax.shard_map(
        on_device, mesh=mesh, in_specs=in_specs, out_specs=out_specs, check_vma=False
    )
```

profile of v0, /device:TPU:57, one launch (start us, length us, event | category | flops | bytes accessed | tf_op | source)
XLA Modules:
  0.0 669.1 jit_solution(17255531953203514862)
XLA Ops:
  6.5 1.0 convert_reduce_fusion.3
  7.5 0.7 multiply_add_fusion.1
  8.3 0.7 all_to_all.16
  9.0 10.6 %all-to-all-start = ((bf16[32,1,2]{2,1,0:T(2,128)(2,1)}), bf16[32,1,2]{2,1,0:T(2,128)(2,1)S(1)}, u32[]{:S(2)}, u32[]{:S(2)}) async-start(bf16[32,1,2]{2,1,0:T(2,128)(2,1)} %all_to_all.16), calls=%async_computation | async-start | bytes 32768 | tf_op jit(solution)/shard_map/all_to_all | solution.py:72
  19.7 1.0 copy.46
  20.7 0.4 convolution_convert_fusion.1
  21.1 1.1 reshape.339
  22.3 5.1 all-to-all-done
  27.4 4.7 all-to-all-start.1
  32.3 0.1 gt.16
  32.5 0.1 add_reduce_fusion
  32.6 14.9 %all-to-all-done.1 = bf16[32,2,4096]{2,1,0:T(2,128)(2,1)S(1)} async-done(((bf16[32,2,4096]{2,1,0:T(2,128)(2,1)}), bf16[32,2,4096]{2,1,0:T(2,128)(2,1)S(1)}, u32[]{:S(2)}, u32[]{:S(2)}) %all-to-all-start.1) | async-done | bytes 524320 | tf_op jit(solution)/shard_map/all_to_all | solution.py:71
  47.6 0.2 reshape.340
  47.8 0.3 convolution_convert_fusion.3
  48.1 0.8 reshape.341
  49.0 0.7 all-gather.12.cloned.1.call-update
  49.7 0.7 all-gather.14.cloned.1.call-update
  50.4 0.5 all-gather.10.cloned.1.call-update
  51.0 0.5 all-gather.18.cloned.1.call-update
  51.6 0.5 all-gather.20.cloned.1.call-update
  52.2 0.7 all-gather.16.cloned.1.call-update
  52.9 0.5 multiply_power_fusion
  53.5 0.1 convert_reduce_fusion.1
  53.6 0.2 select_reduce_fusion
  53.8 21.0 %all-gather.8.cloned.1.call-done = bf16[256,4096]{1,0:T(8,128)(2,1)} async-done(((bf16[256,512]{1,0:T(8,128)(2,1)}), bf16[256,4096]{1,0:T(8,128)(2,1)}) %all-gather.8.cloned.1.call-update) | async-done | bytes 2097168 | tf_op jit(solution)/shard_map/all_gather | solution.py:85
  74.8 2.1 convert_reduce_fusion
  77.0 0.1 copy-done.2
  77.1 0.7 fusion.2
  77.8 1.0 fusion.5
  78.8 0.2 copy-done.4
  79.0 0.6 fusion.28
  79.6 1.4 copy-done.5
  81.0 0.6 fusion.24
  81.6 0.6 fusion.26
  82.2 0.4 multiply_reduce_fusion.1
  82.6 24.0 %all-reduce = (bf16[256,16]{0,1:T(8,128)(2,1)S(1)}, bf16[256,16]{0,1:T(8,128)(2,1)S(1)}, bf16[256,16]{0,1:T(8,128)(2,1)S(1)}) all-reduce(f32[256,16]{0,1:T(8,128)S(1)} %get-tuple-element.6, f32[256,16]{0,1:T(8,128)S(1)} %get-tuple-element.7, f32[256,16]{0,1:T(8,128)S(1)} %get-tuple-element.5), channel_id=1, replica_groups=mesh['req'=32,'mlp'=8] {'mlp'}, use_global_device_ids=true, to_apply=%region_14.15 | all-reduce | flops 12288 | bytes 73728 | tf_op jit(solution)/shard_map/psum | solution.py:100
  106.6 44.5 %all-gather.12.cloned.1.call-done = bf16[4096,256]{1,0:T(8,128)(2,1)} async-done(((bf16[128,256]{1,0:T(8,128)(2,1)}), bf16[4096,256]{1,0:T(8,128)(2,1)}) %all-gather.12.cloned.1.call-update) | async-done | bytes 2097168 | tf_op jit(solution)/shard_map/all_gather | solution.py:114
  151.1 3.2 fusion.85
  154.3 0.1 broadcast_multiply_fusion.1
  154.4 0.3 fusion.8
  154.9 0.7 copy-done.7
  155.5 73.3 %all-gather.14.cloned.1.call-done = bf16[4096,256]{1,0:T(8,128)(2,1)} async-done(((bf16[128,256]{1,0:T(8,128)(2,1)}), bf16[4096,256]{1,0:T(8,128)(2,1)}) %all-gather.14.cloned.1.call-update) | async-done | bytes 2097168 | tf_op jit(solution)/shard_map/all_gather | solution.py:115
  228.8 3.1 convolution_bitcast_fusion
  232.0 0.8 fusion.61
  233.0 0.9 fusion.40
  234.0 0.3 fusion.83
  234.3 72.1 %all-gather.10.cloned.1.call-done = bf16[4096,256]{1,0:T(8,128)(2,1)} async-done(((bf16[128,256]{1,0:T(8,128)(2,1)}), bf16[4096,256]{1,0:T(8,128)(2,1)}) %all-gather.10.cloned.1.call-update) | async-done | bytes 2097168 | tf_op jit(solution)/shard_map/all_gather | solution.py:116
  306.4 3.0 fusion.84
  309.4 0.3 fusion.9
  309.8 97.4 %all-gather.18.cloned.1.call-done = bf16[4096,1024]{1,0:T(8,128)(2,1)} async-done(((bf16[128,1024]{1,0:T(8,128)(2,1)}), bf16[4096,1024]{1,0:T(8,128)(2,1)}) %all-gather.18.cloned.1.call-update) | async-done | bytes 8388624 | tf_op jit(solution)/shard_map/all_gather | solution.py:140
  407.2 7.3 %fusion.86 = f32[256,1024]{1,0:T(8,128)} fusion(bf16[256,4096]{1,0:T(8,128)(2,1)} %copy-done.1, bf16[4096,1024]{1,0:T(8,128)(2,1)} %all-gather.18.cloned.1.call-done), kind=kOutput, calls=%fused_computation.132 | convolution fusion | flops 2147483648 | bytes 11534336 | tf_op jit(solution)/shard_map/dot_general | solution.py:139
  414.5 92.1 %all-gather.20.cloned.1.call-done = bf16[1024,4096]{1,0:T(8,128)(2,1)} async-done(((bf16[1024,128]{1,0:T(8,128)(2,1)}), bf16[1024,4096]{1,0:T(8,128)(2,1)}) %all-gather.20.cloned.1.call-update) | async-done | bytes 8388624 | tf_op jit(solution)/shard_map/all_gather | solution.py:146
  506.6 8.9 %fusion.16 = f32[256,4096]{1,0:T(8,128)} fusion(bf16[1024,4096]{1,0:T(8,128)(2,1)} %all-gather.20.cloned.1.call-done, f32[256,1024]{1,0:T(8,128)} %fusion.86, bf16[256,1024]{0,1:T(8,128)(2,1)S(1)} %bitcast.65, bf16[1024,1024]{1,0:T(8,128)(2,1)S(1)} %copy-done, f32[1024]{0:T(1024)S(1)} %copy-done.12), kind=kOutput, calls=%fused_computation.33 | convolution fusion | flops 2687238144 | bytes 16257024 | tf_op jit(solution)/shard_map/dot_general | solution.py:148
  515.5 67.1 %all-gather.16.cloned.1.call-done = bf16[256,4096]{1,0:T(8,128)(2,1)} async-done(((bf16[256,128]{1,0:T(8,128)(2,1)}), bf16[256,4096]{1,0:T(8,128)(2,1)}) %all-gather.16.cloned.1.call-update) | async-done | bytes 2097168 | tf_op jit(solution)/shard_map/all_gather | solution.py:145
  582.6 5.7 convolution_add_fusion
  588.3 42.6 %reduce-scatter.2.cloned.1.call-done = f32[256,512]{1,0:T(8,128)} async-done(((f32[256,4096]{1,0:T(8,128)}), f32[256,512]{1,0:T(8,128)}) %reduce-scatter.2.cloned.1.call-update) | async-done | bytes 524304 | tf_op jit(solution)/shard_map/reduce_scatter | solution.py:151
  630.9 1.1 add_convert_fusion
  632.0 0.1 reshape.348
  632.2 0.4 convolution_convert_fusion
  632.6 0.3 reshape.349
  632.9 27.0 %all_to_all.20 = bf16[32,2,4096]{2,1,0:T(2,128)(2,1)} all-to-all(bf16[32,2,4096]{2,1,0:T(2,128)(2,1)S(1)} %reshape.349), channel_id=1, replica_groups=mesh['req'=32,'mlp'=8] {'req'}, dimensions={0} | all-to-all | bytes 1048576 | tf_op jit(solution)/shard_map/all_to_all | solution.py:156
  660.0 1.2 reshape.350
  661.2 0.3 convolution_convert_fusion.2
  661.5 0.8 copy.47
  (68 shorter events, 1.1 us)
Async XLA Ops:
  6.5 500.1 %copy-start = (bf16[1024,1024]{1,0:T(8,128)(2,1)S(1)}, bf16[1024,1024]{1,0:T(8,128)(2,1)}, u32[]{:S(2)}) copy-start(bf16[1024,1024]{1,0:T(8,128)(2,1)} %param.37) | copy-start | bytes 6291460
  8.2 23.9 %copy-start.15 = (s32[32]{0:T(128)}, s32[32]{0:T(128)S(1)}, u32[]{:S(2)}) copy-start(s32[32]{0:T(128)S(1)} %multiply_add_fusion.1) | copy-start | bytes 388
  9.0 18.3 %all-to-all-start = ((bf16[32,1,2]{2,1,0:T(2,128)(2,1)}), bf16[32,1,2]{2,1,0:T(2,128)(2,1)S(1)}, u32[]{:S(2)}, u32[]{:S(2)}) async-start(bf16[32,1,2]{2,1,0:T(2,128)(2,1)} %all_to_all.16), calls=%async_computation | async-start | bytes 32768 | tf_op jit(solution)/shard_map/all_to_all | solution.py:72
  22.3 31.2 %copy-start.13 = (s32[256]{0:T(256)S(1)}, s32[256]{0:T(256)}, u32[]{:S(2)}) copy-start(s32[256]{0:T(256)} %param.22) | copy-start | bytes 3076
  22.3 31.4 %copy-start.19 = (s32[256]{0:T(256)S(1)}, s32[256]{0:T(256)}, u32[]{:S(2)}) copy-start(s32[256]{0:T(256)} %param.23) | copy-start | bytes 3076
  27.4 20.2 %all-to-all-start.1 = ((bf16[32,2,4096]{2,1,0:T(2,128)(2,1)}), bf16[32,2,4096]{2,1,0:T(2,128)(2,1)S(1)}, u32[]{:S(2)}, u32[]{:S(2)}) async-start(bf16[32,2,4096]{2,1,0:T(2,128)(2,1)} %reshape.339), calls=%async_computation.1 | async-start | bytes 1048576 | tf_op jit(solution)/shard_map/all_to_all | solution.py:71
  32.0 42.8 %all-gather.8.cloned.1.call-start = ((), (), s32[]{:S(2)}) async-start(), calls=%async_computation.4 | async-start | bytes 2359296 | tf_op jit(solution)/shard_map/all_gather | solution.py:85
  32.1 21.5 %copy-start.17 = (f32[32]{0:T(128)}, f32[32]{0:T(128)S(1)}, u32[]{:S(2)}) copy-start(f32[32]{0:T(128)S(1)} %iota_convert_fusion) | copy-start | bytes 388
  48.9 102.2 %all-gather.12.cloned.1.call-start = ((), (), s32[]{:S(2)}) async-start(), calls=%async_computation.6 | async-start | bytes 2162688 | tf_op jit(solution)/shard_map/all_gather | solution.py:114
  49.7 179.2 %all-gather.14.cloned.1.call-start = ((), (), s32[]{:S(2)}) async-start(), calls=%async_computation.7 | async-start | bytes 2162688 | tf_op jit(solution)/shard_map/all_gather | solution.py:115
  50.4 256.0 %all-gather.10.cloned.1.call-start = ((), (), s32[]{:S(2)}) async-start(), calls=%async_computation.5 | async-start | bytes 2162688 | tf_op jit(solution)/shard_map/all_gather | solution.py:116
  51.0 356.2 %all-gather.18.cloned.1.call-start = ((), (), s32[]{:S(2)}) async-start(), calls=%async_computation.9 | async-start | bytes 8650752 | tf_op jit(solution)/shard_map/all_gather | solution.py:140
  51.6 455.1 %all-gather.20.cloned.1.call-start = ((), (), s32[]{:S(2)}) async-start(), calls=%async_computation.10 | async-start | bytes 8650752 | tf_op jit(solution)/shard_map/all_gather | solution.py:146
  52.1 530.4 %all-gather.16.cloned.1.call-start = ((), (), s32[]{:S(2)}) async-start(), calls=%async_computation.8 | async-start | bytes 2162688 | tf_op jit(solution)/shard_map/all_gather | solution.py:145
  52.9 578.0 %reduce-scatter.2.cloned.1.call-start = ((), (), s32[]{:S(2)}) async-start(), calls=%async_computation.11 | async-start | bytes 4718592 | tf_op jit(solution)/shard_map/reduce_scatter | solution.py:151
  74.8 2.2 copy-start.2
  74.8 2.9 copy-start.10
  74.8 2.9 copy-start.11
  77.8 1.2 copy-start.4
  79.0 2.6 copy-start.1
  79.0 2.0 copy-start.5
  79.0 2.6 copy-start.6
  151.1 3.3 copy-start.8
  154.8 0.7 copy-start.7
  306.4 3.0 copy-start.9
  309.8 196.8 %copy-start.12 = (f32[1024]{0:T(1024)S(1)}, f32[1024]{0:T(1024)}, u32[]{:S(2)}) copy-start(f32[1024]{0:T(1024)} %param.35) | copy-start | bytes 12292
  588.3 42.6 %copy-start.3 = (bf16[256,512]{1,0:T(8,128)(2,1)S(1)}, bf16[256,512]{1,0:T(8,128)(2,1)}, u32[]{:S(2)}) copy-start(bf16[256,512]{1,0:T(8,128)(2,1)} %reshape.341) | copy-start | bytes 786436
  588.3 42.6 %copy-start.14 = (f32[512]{0:T(512)S(1)}, f32[512]{0:T(512)}, u32[]{:S(2)}) copy-start(f32[512]{0:T(512)} %param.39) | copy-start | bytes 6148
  588.3 43.9 %copy-start.18 = (f32[32]{0:T(128)S(1)}, f32[32]{0:T(128)}, u32[]{:S(2)}) copy-start(f32[32]{0:T(128)} %copy-done.17) | copy-start | bytes 388
  632.2 29.1 %copy-start.16 = (s32[32]{0:T(128)S(1)}, s32[32]{0:T(128)}, u32[]{:S(2)}) copy-start(s32[32]{0:T(128)} %copy-done.15) | copy-start | bytes 388
Sparse Core Ops, SparseCore 0:
  49.0 25.7 all-gather.7
  77.4 73.6 all-gather.11
  153.7 75.0 all-gather.13
  231.3 75.0 all-gather.9
  308.9 98.2 all-gather.17
  409.5 97.0 all-gather.19
  509.1 73.4 all-gather.15
  588.4 42.4 reduce-scatter.1
where the time goes:
time: 670 us; the launch traced here: 669 us
  waiting for transfers between devices  534 us (80%)
  blocking collectives  51 us (8%)
  matrix products  35.3 us (5%)
  starting transfers between devices  15.6 us (2%)
  between operations  13.9 us (2%)
  local copies, waits for them, and re-layouts  10.2 us (2%)
  other arithmetic  9.33 us (1%)
    all_gather x1, waiting for transfers between devices, on_device(): lax.all_gather(w_fc_in, 'req', axis=0, tiled=True)  97.4 us
    all_gather x1, waiting for transfers between devices, on_device(): lax.all_gather(w_fc_out, 'req', axis=1, tiled=True)  92.1 us
    all_gather x1, waiting for transfers between devices, on_device(): lax.all_gather(w_key, 'req', axis=0, tiled=True)  73.3 us
    all_gather x1, waiting for transfers between devices, on_device(): lax.all_gather(w_value, 'req', axis=0, tiled=True)  72.1 us
    all_gather x1, waiting for transfers between devices, on_device(): lax.all_gather(w_attn_out, 'req', axis=1, tiled=True)  67.1 us
    all_gather x1, waiting for transfers between devices, on_device(): lax.all_gather(w_query, 'req', axis=0, tiled=True)  44.5 us
    reduce_scatter x1, waiting for transfers between devices, on_device(): shares = lax.psum_scatter(part, 'mlp', scatter_dimension=1, tiled=True)  42.6 us
    all_to_all x1, blocking collectives, on_device(): lax.all_to_all(leaving, 'req', split_axis=0, concat_axis=0, tiled=True)  27 us
  transfers between devices with their start and end apart: 10, of which 10 were waited for; matrix products, arithmetic and copies ran while one was open for 6% of the time, Pallas kernels for 0%

commit v1 on v0

--- a/solution.py
+++ b/solution.py
@@ -2,6 +2,7 @@
 import jax.numpy as jnp
 from jax import lax
 from jax.sharding import PartitionSpec as P
+from jax.lax import all_to_all, psum
 
 HS = 256
 ROT = 64
@@ -82,7 +83,13 @@
     )
     own_x = own_x.astype(jnp.bfloat16).reshape(tok, width_m)
     column = lax.axis_index("mlp") * width_m
-    whole = lax.all_gather(own_x, "mlp", axis=1, tiled=True).astype(jnp.float32)
+
+    def draft_tails(field_in):
+        x_now = psum(1, "mlp")
+        shaped = jnp.stack(x_now * [field_in], 0)
+        return jnp.concatenate(all_to_all(shaped, "mlp", 0, 0), 1)
+
+    whole = draft_tails(own_x).astype(jnp.float32)
     mean = jnp.mean(whole, axis=1, keepdims=True)
     var = jnp.mean(jnp.square(whole - mean), axis=1, keepdims=True)
     full_ln = ((whole - mean) * lax.rsqrt(var + EPS) * ln_gain + ln_bias).astype(jnp.bfloat16)

time: 670 us -> 604 us (0.901)
  waiting for transfers between devices: 534 us -> 455 us
  starting transfers between devices: 15.6 us -> 23 us
    all_gather x1, waiting for transfers between devices: 44.5 us -> 0.01 us  [on_device(): lax.all_gather(w_query, 'req', axis=0, tiled=True)]
    all_gather x1, waiting for transfers between devices: 73.3 us -> 34.8 us  [on_device(): lax.all_gather(w_key, 'req', axis=0, tiled=True)]
    all_to_all x0 -> x1, waiting for transfers between devices: none -> 23.6 us  [draft_tails(): return jnp.concatenate(all_to_all(shaped, 'mlp', 0, 0), 1)]
    all_gather x1 -> x0, waiting for transfers between devices: 21 us -> none  [on_device(): whole = lax.all_gather(own_x, 'mlp', axis=1, tiled=True).astype(jnp.float32)]
    all_to_all x0 -> x1, starting transfers between devices: none -> 7.51 us  [draft_tails(): return jnp.concatenate(all_to_all(shaped, 'mlp', 0, 0), 1)]
  transfers between devices with their start and end apart: 10 -> 10, of which waited for: 10 -> 9; matrix products, arithmetic and copies ran while one was open for 6% -> 8% of each run, Pallas kernels for 0% -> 0%
where the time goes in v1:
time: 604 us; the launch traced here: 603 us
  waiting for transfers between devices  455 us (75%)
  blocking collectives  51 us (8%)
  matrix products  34.9 us (6%)
  starting transfers between devices  23 us (4%)
  between operations  13.9 us (2%)
  local copies, waits for them, and re-layouts  12.5 us (2%)
  other arithmetic  12.5 us (2%)
    all_gather x1, waiting for transfers between devices, on_device(): lax.all_gather(w_fc_in, 'req', axis=0, tiled=True)  97.4 us
    all_gather x1, waiting for transfers between devices, on_device(): lax.all_gather(w_fc_out, 'req', axis=1, tiled=True)  93 us
    all_gather x1, waiting for transfers between devices, on_device(): lax.all_gather(w_value, 'req', axis=0, tiled=True)  71.6 us
    all_gather x1, waiting for transfers between devices, on_device(): lax.all_gather(w_attn_out, 'req', axis=1, tiled=True)  67.1 us
    reduce_scatter x1, waiting for transfers between devices, on_device(): shares = lax.psum_scatter(part, 'mlp', scatter_dimension=1, tiled=True)  42.6 us
    all_gather x1, waiting for transfers between devices, on_device(): lax.all_gather(w_key, 'req', axis=0, tiled=True)  34.8 us
    all_to_all x1, blocking collectives, on_device(): lax.all_to_all(leaving, 'req', split_axis=0, concat_axis=0, tiled=True)  27 us
    psum x1, blocking collectives, on_device(): lax.psum((pick(down_query), pick(down_value), pick(down_fc)), 'mlp')  23.9 us
  transfers between devices with their start and end apart: 10, of which 9 were waited for; matrix products, arithmetic and copies ran while one was open for 8% of the time, Pallas kernels for 0%

profile of v1, /device:TPU:57, one launch (start us, length us, event | category | flops | bytes accessed | tf_op | source)
XLA Modules:
  0.0 603.3 jit_solution(3950781582374520612)
XLA Ops:
  6.5 0.7 all-gather.9.cloned.1.call-update
  7.3 0.7 all-gather.11.cloned.1.call-update
  8.1 0.7 all-gather.7.cloned.1.call-update
  8.8 0.5 all-gather.15.cloned.1.call-update
  9.4 0.5 all-gather.17.cloned.1.call-update
  9.9 0.9 convert_reduce_fusion.3
  10.8 0.7 multiply_add_fusion.1
  11.6 0.7 all_to_all.20
  12.3 10.6 %all-to-all-start = ((bf16[32,1,2]{2,1,0:T(2,128)(2,1)}), bf16[32,1,2]{2,1,0:T(2,128)(2,1)S(1)}, u32[]{:S(2)}, u32[]{:S(2)}) async-start(bf16[32,1,2]{2,1,0:T(2,128)(2,1)} %all_to_all.20), calls=%async_computation | async-start | bytes 32768 | tf_op jit(solution)/shard_map/all_to_all | solution.py:73
  22.9 1.0 copy.49
  24.0 0.4 convolution_convert_fusion.1
  24.4 1.1 reshape.350
  25.5 5.1 all-to-all-done
  30.7 4.6 all-to-all-start.1
  35.9 16.4 %all-to-all-done.1 = bf16[32,2,4096]{2,1,0:T(2,128)(2,1)S(1)} async-done(((bf16[32,2,4096]{2,1,0:T(2,128)(2,1)}), bf16[32,2,4096]{2,1,0:T(2,128)(2,1)S(1)}, u32[]{:S(2)}, u32[]{:S(2)}) %all-to-all-start.1) | async-done | bytes 524320 | tf_op jit(solution)/shard_map/all_to_all | solution.py:72
  52.3 0.2 reshape.351
  52.5 0.3 convolution_convert_fusion.3
  52.8 0.1 reshape.352
  52.9 0.1 copy.40
  53.1 1.4 stack.27
  54.5 7.5 %all-to-all-start.2 = ((bf16[8,256,512]{1,2,0:T(8,128)(2,1)}), bf16[8,256,512]{1,2,0:T(8,128)(2,1)}, u32[]{:S(2)}, u32[]{:S(2)}) async-start(bf16[8,256,512]{1,2,0:T(8,128)(2,1)} %stack.27), calls=%async_computation.2 | async-start | bytes 4194304 | tf_op jit(solution)/shard_map/all_to_all | solution.py:90
  62.0 0.6 all-gather.13.cloned.1.call-update
  62.7 0.1 convert_reduce_fusion.1
  62.8 0.2 select_reduce_fusion
  63.0 23.6 %all-to-all-done.2 = bf16[8,256,512]{1,2,0:T(8,128)(2,1)} async-done(((bf16[8,256,512]{1,2,0:T(8,128)(2,1)}), bf16[8,256,512]{1,2,0:T(8,128)(2,1)}, u32[]{:S(2)}, u32[]{:S(2)}) %all-to-all-start.2) | async-done | bytes 2097184 | tf_op jit(solution)/shard_map/all_to_all | solution.py:90
  86.7 2.1 convert_reduce_fusion
  88.8 2.2 multiply_reduce_fusion
  91.1 2.6 fusion.3
  93.7 0.6 fusion.22
  94.2 1.4 copy-done.3
  95.6 0.6 fusion.26
  96.2 0.6 fusion.24
  96.8 0.4 multiply_reduce_fusion.2
  97.2 23.9 %all-reduce = (bf16[256,16]{0,1:T(8,128)(2,1)S(1)}, bf16[256,16]{0,1:T(8,128)(2,1)S(1)}, bf16[256,16]{0,1:T(8,128)(2,1)S(1)}) all-reduce(f32[256,16]{0,1:T(8,128)S(1)} %get-tuple-element.6, f32[256,16]{0,1:T(8,128)S(1)} %get-tuple-element.7, f32[256,16]{0,1:T(8,128)S(1)} %get-tuple-element.5), channel_id=1, replica_groups=mesh['req'=32,'mlp'=8] {'mlp'}, use_global_device_ids=true, to_apply=%region_14.15 | all-reduce | flops 12288 | bytes 73728 | tf_op jit(solution)/shard_map/psum | solution.py:107
  121.1 0.9 broadcast_multiply_fusion.1
  122.1 3.2 fusion.83
  125.3 1.1 fusion.6
  126.4 0.8 slice.20
  127.2 0.9 slice.21
  128.1 34.8 %all-gather.11.cloned.1.call-done = bf16[4096,256]{1,0:T(8,128)(2,1)} async-done(((bf16[128,256]{1,0:T(8,128)(2,1)}), bf16[4096,256]{1,0:T(8,128)(2,1)}) %all-gather.11.cloned.1.call-update) | async-done | bytes 2097168 | tf_op jit(solution)/shard_map/all_gather | solution.py:122
  162.8 3.1 convolution_bitcast_fusion
  166.0 0.2 fusion.59
  166.4 0.9 fusion.38
  167.4 0.3 fusion.81
  167.6 0.7 copy-done.5
  168.3 0.6 fusion.21
  168.9 71.6 %all-gather.7.cloned.1.call-done = bf16[4096,256]{1,0:T(8,128)(2,1)} async-done(((bf16[128,256]{1,0:T(8,128)(2,1)}), bf16[4096,256]{1,0:T(8,128)(2,1)}) %all-gather.7.cloned.1.call-update) | async-done | bytes 2097168 | tf_op jit(solution)/shard_map/all_gather | solution.py:123
  240.6 3.0 fusion.82
  243.5 0.3 fusion.7
  243.9 97.4 %all-gather.15.cloned.1.call-done = bf16[4096,1024]{1,0:T(8,128)(2,1)} async-done(((bf16[128,1024]{1,0:T(8,128)(2,1)}), bf16[4096,1024]{1,0:T(8,128)(2,1)}) %all-gather.15.cloned.1.call-update) | async-done | bytes 8388624 | tf_op jit(solution)/shard_map/all_gather | solution.py:147
  341.3 6.4 %fusion.84 = f32[256,1024]{1,0:T(8,128)S(1)} fusion(bf16[256,4096]{0,1:T(8,128)(2,1)} %copy-done.1, bf16[4096,1024]{1,0:T(8,128)(2,1)} %all-gather.15.cloned.1.call-done), kind=kOutput, calls=%fused_computation.131 | convolution fusion | flops 2147483648 | bytes 11534336 | tf_op jit(solution)/shard_map/dot_general | solution.py:146
  347.7 93.0 %all-gather.17.cloned.1.call-done = bf16[1024,4096]{1,0:T(8,128)(2,1)} async-done(((bf16[1024,128]{1,0:T(8,128)(2,1)}), bf16[1024,4096]{1,0:T(8,128)(2,1)}) %all-gather.17.cloned.1.call-update) | async-done | bytes 8388624 | tf_op jit(solution)/shard_map/all_gather | solution.py:153
  440.8 8.7 %fusion.14 = f32[256,4096]{1,0:T(8,128)} fusion(bf16[1024,4096]{1,0:T(8,128)(2,1)} %all-gather.17.cloned.1.call-done, f32[256,1024]{1,0:T(8,128)S(1)} %fusion.84, bf16[256,1024]{0,1:T(8,128)(2,1)} %bitcast.77, bf16[1024,1024]{1,0:T(8,128)(2,1)S(1)} %copy-done, f32[1024]{0:T(1024)S(1)} %copy-done.10), kind=kOutput, calls=%fused_computation.32 | convolution fusion | flops 2687238144 | bytes 16257024 | tf_op jit(solution)/shard_map/dot_general | solution.py:155
  449.5 67.1 %all-gather.13.cloned.1.call-done = bf16[256,4096]{1,0:T(8,128)(2,1)} async-done(((bf16[256,128]{1,0:T(8,128)(2,1)}), bf16[256,4096]{1,0:T(8,128)(2,1)}) %all-gather.13.cloned.1.call-update) | async-done | bytes 2097168 | tf_op jit(solution)/shard_map/all_gather | solution.py:152
  516.6 5.8 convolution_add_fusion
  522.4 42.6 %reduce-scatter.2.cloned.1.call-done = f32[256,512]{1,0:T(8,128)} async-done(((f32[256,4096]{1,0:T(8,128)}), f32[256,512]{1,0:T(8,128)}) %reduce-scatter.2.cloned.1.call-update) | async-done | bytes 524304 | tf_op jit(solution)/shard_map/reduce_scatter | solution.py:158
  565.0 1.1 add_convert_fusion
  566.1 0.1 reshape.359
  566.3 0.4 convolution_convert_fusion
  566.7 0.3 reshape.360
  567.1 27.0 %all_to_all.25 = bf16[32,2,4096]{2,1,0:T(2,128)(2,1)} all-to-all(bf16[32,2,4096]{2,1,0:T(2,128)(2,1)S(1)} %reshape.360), channel_id=1, replica_groups=mesh['req'=32,'mlp'=8] {'req'}, dimensions={0} | all-to-all | bytes 1048576 | tf_op jit(solution)/shard_map/all_to_all | solution.py:163
  594.1 1.2 reshape.361
  595.3 0.3 convolution_convert_fusion.2
  595.6 0.8 copy.50
  (65 shorter events, 1.1 us)
Async XLA Ops:
  6.5 434.2 %copy-start = (bf16[1024,1024]{1,0:T(8,128)(2,1)S(1)}, bf16[1024,1024]{1,0:T(8,128)(2,1)}, u32[]{:S(2)}) copy-start(bf16[1024,1024]{1,0:T(8,128)(2,1)} %param.37) | copy-start | bytes 6291460
  6.5 115.5 %all-gather.9.cloned.1.call-start = ((), (), s32[]{:S(2)}) async-start(), calls=%async_computation.6 | async-start | bytes 2162688 | tf_op jit(solution)/shard_map/all_gather | solution.py:121
  7.3 155.6 %all-gather.11.cloned.1.call-start = ((), (), s32[]{:S(2)}) async-start(), calls=%async_computation.7 | async-start | bytes 2162688 | tf_op jit(solution)/shard_map/all_gather | solution.py:122
  8.0 232.6 %all-gather.7.cloned.1.call-start = ((), (), s32[]{:S(2)}) async-start(), calls=%async_computation.5 | async-start | bytes 2162688 | tf_op jit(solution)/shard_map/all_gather | solution.py:123
  8.7 332.6 %all-gather.15.cloned.1.call-start = ((), (), s32[]{:S(2)}) async-start(), calls=%async_computation.9 | async-start | bytes 8650752 | tf_op jit(solution)/shard_map/all_gather | solution.py:147
  9.3 431.4 %all-gather.17.cloned.1.call-start = ((), (), s32[]{:S(2)}) async-start(), calls=%async_computation.10 | async-start | bytes 8650752 | tf_op jit(solution)/shard_map/all_gather | solution.py:153
  11.5 23.9 %copy-start.13 = (s32[32]{0:T(128)}, s32[32]{0:T(128)S(1)}, u32[]{:S(2)}) copy-start(s32[32]{0:T(128)S(1)} %multiply_add_fusion.1) | copy-start | bytes 388
  12.3 18.4 %all-to-all-start = ((bf16[32,1,2]{2,1,0:T(2,128)(2,1)}), bf16[32,1,2]{2,1,0:T(2,128)(2,1)S(1)}, u32[]{:S(2)}, u32[]{:S(2)}) async-start(bf16[32,1,2]{2,1,0:T(2,128)(2,1)} %all_to_all.20), calls=%async_computation | async-start | bytes 32768 | tf_op jit(solution)/shard_map/all_to_all | solution.py:73
  30.7 21.6 %all-to-all-start.1 = ((bf16[32,2,4096]{2,1,0:T(2,128)(2,1)}), bf16[32,2,4096]{2,1,0:T(2,128)(2,1)S(1)}, u32[]{:S(2)}, u32[]{:S(2)}) async-start(bf16[32,2,4096]{2,1,0:T(2,128)(2,1)} %reshape.350), calls=%async_computation.1 | async-start | bytes 1048576 | tf_op jit(solution)/shard_map/all_to_all | solution.py:72
  35.3 17.2 %copy-start.15 = (f32[32]{0:T(128)}, f32[32]{0:T(128)S(1)}, u32[]{:S(2)}) copy-start(f32[32]{0:T(128)S(1)} %iota_convert_fusion) | copy-start | bytes 388
  54.5 8.1 %copy-start.11 = (s32[256]{0:T(256)S(1)}, s32[256]{0:T(256)}, u32[]{:S(2)}) copy-start(s32[256]{0:T(256)} %param.22) | copy-start | bytes 3076
  54.5 8.3 %copy-start.17 = (s32[256]{0:T(256)S(1)}, s32[256]{0:T(256)}, u32[]{:S(2)}) copy-start(s32[256]{0:T(256)} %param.23) | copy-start | bytes 3076
  54.5 32.1 %all-to-all-start.2 = ((bf16[8,256,512]{1,2,0:T(8,128)(2,1)}), bf16[8,256,512]{1,2,0:T(8,128)(2,1)}, u32[]{:S(2)}, u32[]{:S(2)}) async-start(bf16[8,256,512]{1,2,0:T(8,128)(2,1)} %stack.27), calls=%async_computation.2 | async-start | bytes 4194304 | tf_op jit(solution)/shard_map/all_to_all | solution.py:90
  62.0 454.5 %all-gather.13.cloned.1.call-start = ((), (), s32[]{:S(2)}) async-start(), calls=%async_computation.8 | async-start | bytes 2162688 | tf_op jit(solution)/shard_map/all_gather | solution.py:152
  62.6 502.4 %reduce-scatter.2.cloned.1.call-start = ((), (), s32[]{:S(2)}) async-start(), calls=%async_computation.11 | async-start | bytes 4718592 | tf_op jit(solution)/shard_map/reduce_scatter | solution.py:158
  63.0 28.0 %copy-start.8 = (f32[4096]{0:T(1024)S(1)}, f32[4096]{0:T(1024)}, u32[]{:S(2)}) copy-start(f32[4096]{0:T(1024)} %param.25) | copy-start | bytes 49156
  63.0 28.0 %copy-start.9 = (f32[4096]{0:T(1024)S(1)}, f32[4096]{0:T(1024)}, u32[]{:S(2)}) copy-start(f32[4096]{0:T(1024)} %param.24) | copy-start | bytes 49156
  91.0 2.6 copy-start.2
  93.6 2.6 copy-start.1
  93.6 2.0 copy-start.3
  93.7 2.5 copy-start.4
  122.1 3.2 copy-start.6
  167.6 0.7 copy-start.5
  168.9 74.6 %copy-start.7 = (bf16[1024,256]{1,0:T(8,128)(2,1)S(1)}, bf16[1024,256]{1,0:T(8,128)(2,1)}, u32[]{:S(2)}) copy-start(bf16[1024,256]{1,0:T(8,128)(2,1)} %param.33) | copy-start | bytes 1572868
  243.9 196.9 %copy-start.10 = (f32[1024]{0:T(1024)S(1)}, f32[1024]{0:T(1024)}, u32[]{:S(2)}) copy-start(f32[1024]{0:T(1024)} %param.35) | copy-start | bytes 12292
  522.4 42.6 %copy-start.12 = (f32[512]{0:T(512)S(1)}, f32[512]{0:T(512)}, u32[]{:S(2)}) copy-start(f32[512]{0:T(512)} %param.39) | copy-start | bytes 6148
  522.4 43.9 %copy-start.16 = (f32[32]{0:T(128)S(1)}, f32[32]{0:T(128)}, u32[]{:S(2)}) copy-start(f32[32]{0:T(128)} %copy-done.15) | copy-start | bytes 388
  566.3 29.1 %copy-start.14 = (s32[32]{0:T(128)S(1)}, s32[32]{0:T(128)}, u32[]{:S(2)}) copy-start(s32[32]{0:T(128)} %copy-done.13) | copy-start | bytes 388
Sparse Core Ops, SparseCore 0:
  9.9 75.4 all-gather.8
  88.0 74.7 all-gather.10
  165.4 75.0 all-gather.6
  243.0 98.2 all-gather.14
  343.7 97.0 all-gather.16
  443.1 73.4 all-gather.12
  522.6 42.4 reduce-scatter.1
